TPU v7x, 512 devices: a whole 4x4x16 slice. The times are simulated.
512 devices in a mesh: blk: 32 (over z, core), col: 16 (over y, x).
Axes of the slice: x: 4, y: 4, z: 16, core: 2. Of those that a mesh axis runs over, the one named last changes fastest.
Arguments:
- density: float32 [96, 7, 256, 256], P('blk', None, 'col'), as said below
- band_widths: int32 [96], P('blk'), may hold values from 1 to 3, as said below
Outputs:
- purified: float32 [96, 7, 256, 256], P('blk', None, 'col')
Inputs may be any that keep to these rules, and one draw needn't show every extreme that they name: `band_widths`: each block row keeps between 1 and 3 blocks on each side; 3 is reached in every draw. `density`: diagonal entries of the diagonal blocks lie between 0.05 and 0.95, all other entries are small.
All inputs are finite; a program needn't handle non-finite values.
Results may differ from a plain program's by a relative error of at most 0.00013.
Values sent between devices are 32-bit elements; how exact they have to be, the bound alone decides.
No kernel may reach another device: no remote copies, remote signals or barrier semaphores. Data moves between devices by JAX's collectives and lax.ppermute only.
A program may use at most 64 MiB of HBM per device.

v0:
```python
import jax
import jax.numpy as jnp
from jax import lax
from jax.sharding import PartitionSpec as P

W = 3


def send(cells, shift):
    count = lax.axis_size("blk")
    return lax.ppermute(cells, "blk", [(i, (i + shift) % count) for i in range(count)])


def halo_pieces(cells):
    rows = cells.shape[0]
    tail = [cells[rows - W + k, W - k :] for k in range(W)]
    head = [cells[k, : 2 * W - k] for k in range(W)]
    return (tail, head)


def extend(right):
    tail, head = halo_pieces(right)
    from_left = send(jnp.concatenate(tail, axis=0), 1)
    from_right = send(jnp.concatenate(head, axis=0), -1)
    zero = jnp.zeros((1,) + right.shape[2:], right.dtype)
    rows = []
    start = 0
    for k in range(W):
        width = 2 * W + 1 - (W - k)
        piece = from_left[start : start + width]
        start += width
        rows.append(
            jnp.concatenate([jnp.broadcast_to(zero, (W - k,) + right.shape[2:]), piece], axis=0)
        )
    left = jnp.stack(rows)
    rows = []
    start = 0
    for k in range(W):
        width = 2 * W - k
        piece = from_right[start : start + width]
        start += width
        rows.append(
            jnp.concatenate([piece, jnp.broadcast_to(zero, (k + 1,) + right.shape[2:])], axis=0)
        )
    right_rows = jnp.stack(rows)
    return jnp.concatenate([left, right, right_rows], axis=0)


def contract(extended, shard_rows, keep=None):
    local_rows = shard_rows.shape[0]
    span = 2 * W + 1
    zeros = jnp.zeros_like(extended[:local_rows, :1])
    shifted = []
    for inner_band in range(span):
        window = extended[inner_band : inner_band + local_rows]
        shift = inner_band - W
        if shift > 0:
            window = jnp.concatenate([zeros] * shift + [window[:, : span - shift]], axis=1)
        elif shift < 0:
            window = jnp.concatenate([window[:, -shift:]] + [zeros] * -shift, axis=1)
        shifted.append(window)
    stacked = jnp.stack(shifted, axis=3)
    if keep is not None:
        shard_rows = shard_rows * keep
    return jnp.einsum("ibcas,iasr->ibcr", stacked, shard_rows, precision=lax.Precision.HIGH)


def on_device(density, band_widths):
    offsets = jnp.abs(jnp.arange(2 * W + 1, dtype=jnp.int32) - W)
    pattern = (offsets[None, :] <= band_widths[:, None]).astype(jnp.float32)[:, :, None, None]
    current = density * pattern
    for purify_step in range(2):
        if purify_step == 0:
            gathered, keep = (lax.all_gather(density, "col", axis=2, tiled=True), pattern)
        else:
            gathered, keep = (lax.all_gather(current, "col", axis=2, tiled=True), None)
        square = contract(extend(current), gathered, keep) * pattern
        third_power = contract(extend(square), gathered, keep) * pattern
        current = 3.0 * square - 2.0 * third_power
    return current


def solution(mesh):
    in_specs = (P("blk", None, "col", None), P("blk"))
    out_specs = P("blk", None, "col", None)
    return jax.shard_map(
        on_device, mesh=mesh, in_specs=in_specs, out_specs=out_specs, check_vma=False
    )
```

profile of v0, /device:TPU:97, one launch (start us, length us, event | category | flops | bytes accessed | tf_op | source)
XLA Modules:
  0.0 198.5 jit_solution(10707903417032842990)
XLA Ops:
  6.5 0.7 all-gather.3.cloned.1.call-update
  7.3 0.7 compare_convert_fusion
  8.0 1.1 broadcast_multiply_fusion
  9.2 3.4 %collective-permute-start = (f32[15,16,256]{2,1,0:T(8,128)S(1)}, f32[15,16,256]{2,1,0:T(8,128)S(1)}, u32[]{:S(2)}, u32[]{:S(2)}) collective-permute-start(f32[15,16,256]{2,1,0:T(8,128)S(1)} %pad_maximum_fusion), channel_id=1, source_target_pairs={{0,16},{16,32},{32,48},{48,64},{64,80},{80,96},{96,112},{112,128},... | collective-permute-start | bytes 737288 | tf_op jit(solution)/shard_map/ppermute | solution.py:11
  12.7 3.1 %collective-permute-done = f32[15,16,256]{2,1,0:T(8,128)S(1)} collective-permute-done((f32[15,16,256]{2,1,0:T(8,128)S(1)}, f32[15,16,256]{2,1,0:T(8,128)S(1)}, u32[]{:S(2)}, u32[]{:S(2)}) %collective-permute-start) | collective-permute-done | bytes 245792 | tf_op jit(solution)/shard_map/ppermute | solution.py:11
  15.8 3.7 %collective-permute-done.1 = f32[15,16,256]{2,1,0:T(8,128)S(1)} collective-permute-done((f32[15,16,256]{2,1,0:T(8,128)S(1)}, f32[15,16,256]{2,1,0:T(8,128)S(1)}, u32[]{:S(2)}, u32[]{:S(2)}) %collective-permute-start.1) | collective-permute-done | bytes 245792 | tf_op jit(solution)/shard_map/ppermute | solution.py:11
  19.7 0.1 fusion.84
  19.8 0.1 bitcast_dynamic-update-slice_fusion
  20.0 66.8 %all-gather.3.cloned.1.call-done = f32[3,7,256,256]{3,2,1,0:T(8,128)} async-done(((f32[3,7,16,256]{3,2,1,0:T(8,128)}), f32[3,7,256,256]{3,2,1,0:T(8,128)}) %all-gather.3.cloned.1.call-update) | async-done | bytes 5505040 | tf_op jit(solution)/shard_map/all_gather | solution.py:74
  86.8 4.4 %fusion.16 = f32[3,7,16,256]{3,2,1,0:T(8,128)S(1)} fusion(f32[3,7,16,7,256]{4,2,3,1,0:T(8,128)S(1)} %fusion.68, f32[3,7,256,256]{3,2,1,0:T(8,128)} %all-gather.3.cloned.1.call-done, f32[3,7]{1,0:T(4,128)S(1)} %compare_convert_fusion), kind=kOutput, calls=%fused_computation.15 | convolution fusion | flops 926306304 | bytes 8257620 | tf_op jit(solution)/shard_map/ibcas,iasr->ibcr/dot_general | solution.py:65
  91.3 3.1 %collective-permute-start.2 = (f32[15,16,256]{2,1,0:T(8,128)S(1)}, f32[15,16,256]{2,1,0:T(8,128)S(1)}, u32[]{:S(2)}, u32[]{:S(2)}) collective-permute-start(f32[15,16,256]{2,1,0:T(8,128)S(1)} %pad_maximum_fusion.2), channel_id=1, source_target_pairs={{0,16},{16,32},{32,48},{48,64},{64,80},{80,96},{96,112},{112,128},... | collective-permute-start | bytes 737288 | tf_op jit(solution)/shard_map/ppermute | solution.py:11
  94.4 3.1 %collective-permute-done.2 = f32[15,16,256]{2,1,0:T(8,128)S(1)} collective-permute-done((f32[15,16,256]{2,1,0:T(8,128)S(1)}, f32[15,16,256]{2,1,0:T(8,128)S(1)}, u32[]{:S(2)}, u32[]{:S(2)}) %collective-permute-start.2) | collective-permute-done | bytes 245792 | tf_op jit(solution)/shard_map/ppermute | solution.py:11
  97.7 3.5 %collective-permute-done.3 = f32[15,16,256]{2,1,0:T(8,128)S(1)} collective-permute-done((f32[15,16,256]{2,1,0:T(8,128)S(1)}, f32[15,16,256]{2,1,0:T(8,128)S(1)}, u32[]{:S(2)}, u32[]{:S(2)}) %collective-permute-start.3) | collective-permute-done | bytes 245792 | tf_op jit(solution)/shard_map/ppermute | solution.py:11
  101.5 1.7 fusion.2
  103.2 0.8 fusion.80
  104.0 0.9 slice_bitcast_fusion.18
  105.0 1.0 slice_bitcast_fusion.10
  106.0 1.0 slice_bitcast_fusion.2
  106.9 0.2 collective-permute-start.4
  107.2 0.3 collective-permute-start.5
  107.5 2.8 %collective-permute-done.4 = f32[15,16,256]{2,1,0:T(8,128)S(1)} collective-permute-done((f32[15,16,256]{2,1,0:T(8,128)S(1)}, f32[15,16,256]{2,1,0:T(8,128)S(1)}, u32[]{:S(2)}, u32[]{:S(2)}) %collective-permute-start.4) | collective-permute-done | bytes 245792 | tf_op jit(solution)/shard_map/ppermute | solution.py:11
  110.3 3.7 %collective-permute-done.5 = f32[15,16,256]{2,1,0:T(8,128)S(1)} collective-permute-done((f32[15,16,256]{2,1,0:T(8,128)S(1)}, f32[15,16,256]{2,1,0:T(8,128)S(1)}, u32[]{:S(2)}, u32[]{:S(2)}) %collective-permute-start.5) | collective-permute-done | bytes 245792 | tf_op jit(solution)/shard_map/ppermute | solution.py:11
  114.2 0.1 fusion.82
  114.4 59.8 %all-gather.5.cloned.1.call-done = f32[3,7,256,256]{3,2,1,0:T(8,128)} async-done(((f32[3,7,16,256]{3,2,1,0:T(8,128)}), f32[3,7,256,256]{3,2,1,0:T(8,128)}) %all-gather.5.cloned.1.call-update) | async-done | bytes 5505040 | tf_op jit(solution)/shard_map/all_gather | solution.py:76
  174.2 4.4 %fusion.6 = f32[3,7,16,256,1]{3,2,0,1,4:T(8,128)S(1)} fusion(f32[3,7,16,7,256]{4,2,1,0,3:T(8,128)S(1)} %fusion.32, f32[3,7,256,256]{3,2,1,0:T(8,128)} %all-gather.5.cloned.1.call-done), kind=kOutput, calls=%fused_computation.6 | convolution fusion | flops 924844032 | bytes 8257536 | tf_op jit(solution)/shard_map/ibcas,iasr->ibcr/dot_general | solution.py:65
  178.7 0.1 bitcast_multiply_fusion.1
  178.9 3.1 %collective-permute-start.6 = (f32[15,16,256]{2,1,0:T(8,128)S(1)}, f32[15,16,256]{2,1,0:T(8,128)S(1)}, u32[]{:S(2)}, u32[]{:S(2)}) collective-permute-start(f32[15,16,256]{2,1,0:T(8,128)S(1)} %pad_maximum_fusion.6), channel_id=1, source_target_pairs={{0,16},{16,32},{32,48},{48,64},{64,80},{80,96},{96,112},{112,128},... | collective-permute-start | bytes 737288 | tf_op jit(solution)/shard_map/ppermute | solution.py:11
  182.0 3.1 %collective-permute-done.6 = f32[15,16,256]{2,1,0:T(8,128)S(1)} collective-permute-done((f32[15,16,256]{2,1,0:T(8,128)S(1)}, f32[15,16,256]{2,1,0:T(8,128)S(1)}, u32[]{:S(2)}, u32[]{:S(2)}) %collective-permute-start.6) | collective-permute-done | bytes 245792 | tf_op jit(solution)/shard_map/ppermute | solution.py:11
  185.2 0.1 bitcast_dynamic-update-slice_fusion.1
  185.3 3.4 %collective-permute-done.7 = f32[15,16,256]{2,1,0:T(8,128)S(1)} collective-permute-done((f32[15,16,256]{2,1,0:T(8,128)S(1)}, f32[15,16,256]{2,1,0:T(8,128)S(1)}, u32[]{:S(2)}, u32[]{:S(2)}) %collective-permute-start.7) | collective-permute-done | bytes 245792 | tf_op jit(solution)/shard_map/ppermute | solution.py:11
  189.0 1.8 fusion.4
  190.8 0.9 fusion.78
  (106 shorter events, 1.5 us)
Async XLA Ops:
  6.5 80.2 %all-gather.3.cloned.1.call-start = ((), (), s32[]{:S(2)}) async-start(), calls=%async_computation | async-start | bytes 5849088 | tf_op jit(solution)/shard_map/all_gather | solution.py:74
  7.3 167.0 %all-gather.5.cloned.1.call-start = ((), (), s32[]{:S(2)}) async-start(), calls=%async_computation.1 | async-start | bytes 5849088 | tf_op jit(solution)/shard_map/all_gather | solution.py:76
  9.2 10.5 %copy-start.2 = (pred[7]{0:T(512)(128)(4,1)S(1)}, pred[7]{0:T(512)(128)(4,1)}, u32[]{:S(2)}) copy-start(pred[7]{0:T(512)(128)(4,1)} %constant.7.clone.1) | copy-start | bytes 25
  9.2 6.6 %collective-permute-start = (f32[15,16,256]{2,1,0:T(8,128)S(1)}, f32[15,16,256]{2,1,0:T(8,128)S(1)}, u32[]{:S(2)}, u32[]{:S(2)}) collective-permute-start(f32[15,16,256]{2,1,0:T(8,128)S(1)} %pad_maximum_fusion), channel_id=1, source_target_pairs={{0,16},{16,32},{32,48},{48,64},{64,80},{80,96},{96,112},{112,128},... | collective-permute-start | bytes 737288 | tf_op jit(solution)/shard_map/ppermute | solution.py:11
  12.6 7.1 %copy-start.1 = (f32[3,7,16,256]{3,2,1,0:T(8,128)S(1)}, f32[3,7,16,256]{3,2,1,0:T(8,128)}, u32[]{:S(2)}) copy-start(f32[3,7,16,256]{3,2,1,0:T(8,128)} %param.2) | copy-start | bytes 1032196
  12.7 6.8 %collective-permute-start.1 = (f32[15,16,256]{2,1,0:T(8,128)S(1)}, f32[15,16,256]{2,1,0:T(8,128)S(1)}, u32[]{:S(2)}, u32[]{:S(2)}) collective-permute-start(f32[15,16,256]{2,1,0:T(8,128)S(1)} %pad_maximum_fusion.1), channel_id=1, source_target_pairs={{0,496},{16,0},{32,16},{48,32},{64,48},{80,64},{96,80},{112,96},{1... | collective-permute-start | bytes 737288 | tf_op jit(solution)/shard_map/ppermute | solution.py:11
  86.8 14.7 %slice-start = ((s8[5505024]{0:T(1024)(128)(4,1)}), s8[4194304]{0:T(1024)(128)(4,1)S(1)}, s32[]{:S(2)}) async-start(s8[5505024]{0:T(1024)(128)(4,1)} %bitcast.255), calls=%async_computation.2 | async-start | bytes 8388608
  91.2 10.2 %slice-start.1 = ((s8[5505024]{0:T(1024)(128)(4,1)}), s8[1310720]{0:T(1024)(128)(4,1)S(1)}, s32[]{:S(2)}) async-start(s8[5505024]{0:T(1024)(128)(4,1)} %bitcast.255), calls=%async_computation.3 | async-start | bytes 2621440
  91.3 6.2 %collective-permute-start.2 = (f32[15,16,256]{2,1,0:T(8,128)S(1)}, f32[15,16,256]{2,1,0:T(8,128)S(1)}, u32[]{:S(2)}, u32[]{:S(2)}) collective-permute-start(f32[15,16,256]{2,1,0:T(8,128)S(1)} %pad_maximum_fusion.2), channel_id=1, source_target_pairs={{0,16},{16,32},{32,48},{48,64},{64,80},{80,96},{96,112},{112,128},... | collective-permute-start | bytes 737288 | tf_op jit(solution)/shard_map/ppermute | solution.py:11
  94.4 6.8 %collective-permute-start.3 = (f32[15,16,256]{2,1,0:T(8,128)S(1)}, f32[15,16,256]{2,1,0:T(8,128)S(1)}, u32[]{:S(2)}, u32[]{:S(2)}) collective-permute-start(f32[15,16,256]{2,1,0:T(8,128)S(1)} %pad_maximum_fusion.3), channel_id=1, source_target_pairs={{0,496},{16,0},{32,16},{48,32},{64,48},{80,64},{96,80},{112,96},{1... | collective-permute-start | bytes 737288 | tf_op jit(solution)/shard_map/ppermute | solution.py:11
  104.0 10.1 %copy-start = (f32[3,7,16,256]{3,2,1,0:T(8,128)S(1)}, f32[3,7,16,256]{3,2,1,0:T(8,128)}, u32[]{:S(2)}) copy-start(f32[3,7,16,256]{3,2,1,0:T(8,128)} %fusion.80) | copy-start | bytes 1032196
  106.9 3.4 %collective-permute-start.4 = (f32[15,16,256]{2,1,0:T(8,128)S(1)}, f32[15,16,256]{2,1,0:T(8,128)S(1)}, u32[]{:S(2)}, u32[]{:S(2)}) collective-permute-start(f32[15,16,256]{2,1,0:T(8,128)S(1)} %pad_maximum_fusion.4), channel_id=1, source_target_pairs={{0,16},{16,32},{32,48},{48,64},{64,80},{80,96},{96,112},{112,128},... | collective-permute-start | bytes 737288 | tf_op jit(solution)/shard_map/ppermute | solution.py:11
  107.2 6.8 %collective-permute-start.5 = (f32[15,16,256]{2,1,0:T(8,128)S(1)}, f32[15,16,256]{2,1,0:T(8,128)S(1)}, u32[]{:S(2)}, u32[]{:S(2)}) collective-permute-start(f32[15,16,256]{2,1,0:T(8,128)S(1)} %pad_maximum_fusion.5), channel_id=1, source_target_pairs={{0,496},{16,0},{32,16},{48,32},{64,48},{80,64},{96,80},{112,96},{1... | collective-permute-start | bytes 737288 | tf_op jit(solution)/shard_map/ppermute | solution.py:11
  174.2 14.8 %slice-start.2 = ((s8[5505024]{0:T(1024)(128)(4,1)}), s8[4194304]{0:T(1024)(128)(4,1)S(1)}, s32[]{:S(2)}) async-start(s8[5505024]{0:T(1024)(128)(4,1)} %bitcast.257), calls=%async_computation.4 | async-start | bytes 8388608
  178.8 10.3 %slice-start.3 = ((s8[5505024]{0:T(1024)(128)(4,1)}), s8[1310720]{0:T(1024)(128)(4,1)S(1)}, s32[]{:S(2)}) async-start(s8[5505024]{0:T(1024)(128)(4,1)} %bitcast.257), calls=%async_computation.5 | async-start | bytes 2621440
  178.9 6.2 %collective-permute-start.6 = (f32[15,16,256]{2,1,0:T(8,128)S(1)}, f32[15,16,256]{2,1,0:T(8,128)S(1)}, u32[]{:S(2)}, u32[]{:S(2)}) collective-permute-start(f32[15,16,256]{2,1,0:T(8,128)S(1)} %pad_maximum_fusion.6), channel_id=1, source_target_pairs={{0,16},{16,32},{32,48},{48,64},{64,80},{80,96},{96,112},{112,128},... | collective-permute-start | bytes 737288 | tf_op jit(solution)/shard_map/ppermute | solution.py:11
  181.9 6.8 %collective-permute-start.7 = (f32[15,16,256]{2,1,0:T(8,128)S(1)}, f32[15,16,256]{2,1,0:T(8,128)S(1)}, u32[]{:S(2)}, u32[]{:S(2)}) collective-permute-start(f32[15,16,256]{2,1,0:T(8,128)S(1)} %pad_maximum_fusion.7), channel_id=1, source_target_pairs={{0,496},{16,0},{32,16},{48,32},{64,48},{80,64},{96,80},{112,96},{1... | collective-permute-start | bytes 737288 | tf_op jit(solution)/shard_map/ppermute | solution.py:11
Sparse Core Ops, SparseCore 0:
  10.4 76.3 all-gather.2
  104.2 70.0 all-gather.4
where the time goes:
time: 199 us; the launch traced here: 198 us
  waiting for transfers between devices  154 us (77%)
  between operations  14.1 us (7%)
  matrix products  12.3 us (6%)
  starting transfers between devices  10.2 us (5%)
  other arithmetic  4.81 us (2%)
  local copies, waits for them, and re-layouts  3.36 us (2%)
    all_gather x1, waiting for transfers between devices, on_device(): lax.all_gather(density, 'col', axis=2, tiled=True)  66.8 us
    all_gather x1, waiting for transfers between devices, on_device(): gathered, keep = (lax.all_gather(current, 'col', axis=2, tiled=True), None)  59.8 us
    ppermute x8, waiting for transfers between devices, send(): lax.ppermute(cells, 'blk', [(i, (i + shift) % count) for i in range(count)])  26.4 us
    dot_general x4, matrix products, contract(): jnp.einsum('ibcas,iasr->ibcr', stacked, shard_rows, precision=lax.Precisi...  12.3 us
    ppermute x8, starting transfers between devices, send(): lax.ppermute(cells, 'blk', [(i, (i + shift) % count) for i in range(count)])  10.1 us
  transfers between devices with their start and end apart: 10, of which 10 were waited for; matrix products, arithmetic and copies ran while one was open for 3% of the time, Pallas kernels for 0%

commit v1 on v0

--- a/solution.py
+++ b/solution.py
@@ -2,8 +2,33 @@
 import jax.numpy as jnp
 from jax import lax
 from jax.sharding import PartitionSpec as P
+from jax.lax import axis_index, axis_size, ppermute
 
 W = 3
+
+
+def cover_the_knots(payload):
+    arr_next, w_next, odd = (axis_size("col"), axis_index("col"), payload.shape[2])
+    h_now = map(lambda u: (u, (u + 1) % arr_next), range(arr_next))
+    frames = list(h_now)
+    everything = range(arr_next)
+    passed = map(lambda u: (u, (u - 1) % arr_next), everything)
+    gallery = list(passed)
+    out_arr = jnp.zeros((*payload.shape[:2], arr_next * odd, *payload.shape[3:]), payload.dtype)
+    out_arr = lax.dynamic_update_slice_in_dim(out_arr, payload, w_next * odd, axis=2)
+    kept_arr = opened = payload
+    far_arr = arr_next // 2
+    for idx in range(1, far_arr + 1):
+        kept_arr = ppermute(kept_arr, "col", frames)
+        out_arr = lax.dynamic_update_slice_in_dim(
+            out_arr, kept_arr, (w_next - idx) % arr_next * odd, axis=2
+        )
+        if idx < arr_next - far_arr:
+            opened = ppermute(opened, axis_name="col", perm=gallery)
+            out_arr = lax.dynamic_update_slice_in_dim(
+                out_arr, opened, (w_next + idx) % arr_next * odd, axis=2
+            )
+    return out_arr
 
 
 def send(cells, shift):
@@ -71,7 +96,7 @@
     current = density * pattern
     for purify_step in range(2):
         if purify_step == 0:
-            gathered, keep = (lax.all_gather(density, "col", axis=2, tiled=True), pattern)
+            gathered, keep = (cover_the_knots(density), pattern)
         else:
             gathered, keep = (lax.all_gather(current, "col", axis=2, tiled=True), None)
         square = contract(extend(current), gathered, keep) * pattern

time: 199 us -> 234 us (1.18)
  starting transfers between devices: 10.2 us -> 76.1 us
  waiting for transfers between devices: 154 us -> 106 us
  local copies, waits for them, and re-layouts: 3.36 us -> 18.1 us
  matrix products: 12.3 us -> 14.7 us
    all_gather x1 -> x0, waiting for transfers between devices: 66.8 us -> none  [on_device(): lax.all_gather(density, 'col', axis=2, tiled=True)]
    ppermute x0 -> x15, starting transfers between devices: none -> 62.1 us  [the longest x7 45.4 us: cover_the_knots(): opened = ppermute(opened, axis_name='col', perm=gallery)]
    ppermute x0 -> x15, waiting for transfers between devices: none -> 30 us  [the longest x8 29.9 us: cover_the_knots(): kept_arr = ppermute(kept_arr, 'col', frames)]
    dynamic_update_slice x0 -> x15, local copies, waits for them, and re-layouts: none -> 11.7 us  [the longest x8 6.22 us: cover_the_knots(): lax.dynamic_update_slice_in_dim(out_arr, kept_arr, (w_next - idx) % arr_n...]
    ppermute x8, waiting for transfers between devices: 26.4 us -> 20.6 us  [send(): lax.ppermute(cells, 'blk', [(i, (i + shift) % count) for i in range(count)])]
    all_gather x1, waiting for transfers between devices: 59.8 us -> 55.2 us  [on_device(): gathered, keep = (lax.all_gather(current, 'col', axis=2, tiled=True), None)]
    ppermute x8, starting transfers between devices: 10.1 us -> 14 us  [send(): lax.ppermute(cells, 'blk', [(i, (i + shift) % count) for i in range(count)])]
    broadcast_in_dim x0 -> x1, local copies, waits for them, and re-layouts: none -> 3.02 us  [cover_the_knots(): jnp.zeros((*payload.shape[:2], arr_next * odd, *payload.shape[3:]), paylo...]
  transfers between devices with their start and end apart: 10 -> 24, of which waited for: 10 -> 17; matrix products, arithmetic and copies ran while one was open for 3% -> 6% of each run, Pallas kernels for 0% -> 0%
where the time goes in v1:
time: 234 us
  waiting for transfers between devices  106 us (45%)
  starting transfers between devices  76.1 us (33%)
  local copies, waits for them, and re-layouts  18.1 us (8%)
  matrix products  14.7 us (6%)
  between operations  14.5 us (6%)
  other arithmetic  4.52 us (2%)
    all_gather x1, waiting for transfers between devices, on_device(): gathered, keep = (lax.all_gather(current, 'col', axis=2, tiled=True), None)  55.2 us
    ppermute x7, starting transfers between devices, cover_the_knots(): opened = ppermute(opened, axis_name='col', perm=gallery)  45.4 us
    ppermute x8, waiting for transfers between devices, cover_the_knots(): kept_arr = ppermute(kept_arr, 'col', frames)  29.9 us
    ppermute x8, waiting for transfers between devices, send(): lax.ppermute(cells, 'blk', [(i, (i + shift) % count) for i in range(count)])  20.6 us
    ppermute x8, starting transfers between devices, cover_the_knots(): kept_arr = ppermute(kept_arr, 'col', frames)  16.6 us
    dot_general x4, matrix products, contract(): jnp.einsum('ibcas,iasr->ibcr', stacked, shard_rows, precision=lax.Precisi...  14.7 us
    ppermute x8, starting transfers between devices, send(): lax.ppermute(cells, 'blk', [(i, (i + shift) % count) for i in range(count)])  14 us
    dynamic_update_slice x8, local copies, waits for them, and re-layouts, cover_the_knots(): lax.dynamic_update_slice_in_dim(out_arr, kept_arr, (w_next - idx) % arr_n...  6.22 us
  transfers between devices with their start and end apart: 24, of which 17 were waited for; matrix products, arithmetic and copies ran while one was open for 6% of the time, Pallas kernels for 0%

profile of v1, /device:TPU:97, one launch (start us, length us, event | category | flops | bytes accessed | tf_op | source)
XLA Modules:
  0.0 233.7 jit_solution(14194893266792425303)
XLA Ops:
  7.3 3.0 %broadcast_in_dim.2 = f32[3,7,256,256]{3,2,1,0:T(8,128)} broadcast(f32[]{:T(128)} %constant.103.clone.1), dimensions={} | broadcast | bytes 5505028 | tf_op jit(solution)/shard_map/broadcast_in_dim | solution.py:17
  11.2 3.4 %collective-permute-start = (f32[15,16,256]{2,1,0:T(8,128)S(1)}, f32[15,16,256]{2,1,0:T(8,128)S(1)}, u32[]{:S(2)}, u32[]{:S(2)}) collective-permute-start(f32[15,16,256]{2,1,0:T(8,128)S(1)} %pad_maximum_fusion), channel_id=1, source_target_pairs={{0,16},{16,32},{32,48},{48,64},{64,80},{80,96},{96,112},{112,128},... | collective-permute-start | bytes 737288 | tf_op jit(solution)/shard_map/ppermute | solution.py:36
  14.7 3.1 %collective-permute-start.2 = (f32[3,7,16,256]{3,2,1,0:T(8,128)S(1)}, f32[3,7,16,256]{3,2,1,0:T(8,128)S(1)}, u32[]{:S(2)}, u32[]{:S(2)}) collective-permute-start(f32[3,7,16,256]{3,2,1,0:T(8,128)S(1)} %copy-done.1), channel_id=1, source_target_pairs={{0,1},{1,2},{2,3},{3,4},{4,5},{5,6},{6,7},{7,8},{8,9},{9,10},{10,1... | collective-permute-start | bytes 1032200 | tf_op jit(solution)/shard_map/ppermute | solution.py:22
  17.8 5.6 %collective-permute-start.3 = (f32[3,7,16,256]{3,2,1,0:T(8,128)S(1)}, f32[3,7,16,256]{3,2,1,0:T(8,128)S(1)}, u32[]{:S(2)}, u32[]{:S(2)}) collective-permute-start(f32[3,7,16,256]{3,2,1,0:T(8,128)S(1)} %copy-done.1), channel_id=1, source_target_pairs={{0,15},{1,0},{2,1},{3,2},{4,3},{5,4},{6,5},{7,6},{8,7},{9,8},{10,9... | collective-permute-start | bytes 1032200 | tf_op jit(solution)/shard_map/ppermute | solution.py:27
  23.9 3.5 %collective-permute-done.2 = f32[3,7,16,256]{3,2,1,0:T(8,128)S(1)} collective-permute-done((f32[3,7,16,256]{3,2,1,0:T(8,128)S(1)}, f32[3,7,16,256]{3,2,1,0:T(8,128)S(1)}, u32[]{:S(2)}, u32[]{:S(2)}) %collective-permute-start.2) | collective-permute-done | bytes 344096 | tf_op jit(solution)/shard_map/ppermute | solution.py:22
  27.4 1.9 collective-permute-start.4
  30.3 6.0 %collective-permute-start.5 = (f32[3,7,16,256]{3,2,1,0:T(8,128)S(1)}, f32[3,7,16,256]{3,2,1,0:T(8,128)S(1)}, u32[]{:S(2)}, u32[]{:S(2)}) collective-permute-start(f32[3,7,16,256]{3,2,1,0:T(8,128)S(1)} %collective-permute-done.3), channel_id=1, source_target_pairs={{0,15},{1,0},{2,1},{3,2},{4,3},{5,4},{6,5},{7,6},{8,7},{9,8},{10,9... | collective-permute-start | bytes 1032200 | tf_op jit(solution)/shard_map/ppermute | solution.py:27
  36.4 4.7 %collective-permute-done.4 = f32[3,7,16,256]{3,2,1,0:T(8,128)S(1)} collective-permute-done((f32[3,7,16,256]{3,2,1,0:T(8,128)S(1)}, f32[3,7,16,256]{3,2,1,0:T(8,128)S(1)}, u32[]{:S(2)}, u32[]{:S(2)}) %collective-permute-start.4) | collective-permute-done | bytes 344096 | tf_op jit(solution)/shard_map/ppermute | solution.py:22
  41.1 1.9 collective-permute-start.6
  43.1 7.1 %collective-permute-start.7 = (f32[3,7,16,256]{3,2,1,0:T(8,128)S(1)}, f32[3,7,16,256]{3,2,1,0:T(8,128)S(1)}, u32[]{:S(2)}, u32[]{:S(2)}) collective-permute-start(f32[3,7,16,256]{3,2,1,0:T(8,128)S(1)} %collective-permute-done.5), channel_id=1, source_target_pairs={{0,15},{1,0},{2,1},{3,2},{4,3},{5,4},{6,5},{7,6},{8,7},{9,8},{10,9... | collective-permute-start | bytes 1032200 | tf_op jit(solution)/shard_map/ppermute | solution.py:27
  50.3 5.7 %collective-permute-done.6 = f32[3,7,16,256]{3,2,1,0:T(8,128)S(1)} collective-permute-done((f32[3,7,16,256]{3,2,1,0:T(8,128)S(1)}, f32[3,7,16,256]{3,2,1,0:T(8,128)S(1)}, u32[]{:S(2)}, u32[]{:S(2)}) %collective-permute-start.6) | collective-permute-done | bytes 344096 | tf_op jit(solution)/shard_map/ppermute | solution.py:22
  56.0 1.9 collective-permute-start.8
  58.7 6.7 %collective-permute-start.9 = (f32[3,7,16,256]{3,2,1,0:T(8,128)S(1)}, f32[3,7,16,256]{3,2,1,0:T(8,128)S(1)}, u32[]{:S(2)}, u32[]{:S(2)}) collective-permute-start(f32[3,7,16,256]{3,2,1,0:T(8,128)S(1)} %collective-permute-done.7), channel_id=1, source_target_pairs={{0,15},{1,0},{2,1},{3,2},{4,3},{5,4},{6,5},{7,6},{8,7},{9,8},{10,9... | collective-permute-start | bytes 1032200 | tf_op jit(solution)/shard_map/ppermute | solution.py:27
  66.2 4.2 %collective-permute-done.8 = f32[3,7,16,256]{3,2,1,0:T(8,128)S(1)} collective-permute-done((f32[3,7,16,256]{3,2,1,0:T(8,128)S(1)}, f32[3,7,16,256]{3,2,1,0:T(8,128)S(1)}, u32[]{:S(2)}, u32[]{:S(2)}) %collective-permute-start.8) | collective-permute-done | bytes 344096 | tf_op jit(solution)/shard_map/ppermute | solution.py:22
  73.9 6.7 %collective-permute-start.11 = (f32[3,7,16,256]{3,2,1,0:T(8,128)S(1)}, f32[3,7,16,256]{3,2,1,0:T(8,128)S(1)}, u32[]{:S(2)}, u32[]{:S(2)}) collective-permute-start(f32[3,7,16,256]{3,2,1,0:T(8,128)S(1)} %collective-permute-done.9), channel_id=1, source_target_pairs={{0,15},{1,0},{2,1},{3,2},{4,3},{5,4},{6,5},{7,6},{8,7},{9,8},{10,9... | collective-permute-start | bytes 1032200 | tf_op jit(solution)/shard_map/ppermute | solution.py:27
  81.4 2.6 %collective-permute-done.10 = f32[3,7,16,256]{3,2,1,0:T(8,128)S(1)} collective-permute-done((f32[3,7,16,256]{3,2,1,0:T(8,128)S(1)}, f32[3,7,16,256]{3,2,1,0:T(8,128)S(1)}, u32[]{:S(2)}, u32[]{:S(2)}) %collective-permute-start.10) | collective-permute-done | bytes 344096 | tf_op jit(solution)/shard_map/ppermute | solution.py:22
  87.4 6.7 %collective-permute-start.13 = (f32[3,7,16,256]{3,2,1,0:T(8,128)S(1)}, f32[3,7,16,256]{3,2,1,0:T(8,128)S(1)}, u32[]{:S(2)}, u32[]{:S(2)}) collective-permute-start(f32[3,7,16,256]{3,2,1,0:T(8,128)S(1)} %collective-permute-done.11), channel_id=1, source_target_pairs={{0,15},{1,0},{2,1},{3,2},{4,3},{5,4},{6,5},{7,6},{8,7},{9,8},{10,9... | collective-permute-start | bytes 1032200 | tf_op jit(solution)/shard_map/ppermute | solution.py:27
  100.0 6.7 %collective-permute-start.15 = (f32[3,7,16,256]{3,2,1,0:T(8,128)S(1)}, f32[3,7,16,256]{3,2,1,0:T(8,128)S(1)}, u32[]{:S(2)}, u32[]{:S(2)}) collective-permute-start(f32[3,7,16,256]{3,2,1,0:T(8,128)S(1)} %collective-permute-done.13), channel_id=1, source_target_pairs={{0,15},{1,0},{2,1},{3,2},{4,3},{5,4},{6,5},{7,6},{8,7},{9,8},{10,9... | collective-permute-start | bytes 1032200 | tf_op jit(solution)/shard_map/ppermute | solution.py:27
  108.2 2.1 collective-permute-start.16
  112.7 6.8 %collective-permute-done.16 = f32[3,7,16,256]{3,2,1,0:T(8,128)S(1)} collective-permute-done((f32[3,7,16,256]{3,2,1,0:T(8,128)S(1)}, f32[3,7,16,256]{3,2,1,0:T(8,128)S(1)}, u32[]{:S(2)}, u32[]{:S(2)}) %collective-permute-start.16) | collective-permute-done | bytes 344096 | tf_op jit(solution)/shard_map/ppermute | solution.py:22
  120.3 4.3 %fusion.16 = f32[3,7,16,256]{3,2,1,0:T(8,128)S(1)} fusion(f32[3,7,16,7,256]{4,2,3,1,0:T(8,128)S(1)} %fusion.68, f32[3,7,256,256]{3,2,1,0:T(8,128)} %constant_dynamic-update-slice_fusion, f32[3,7]{1,0:T(4,128)S(1)} %compare_convert_fusion), kind=kOutput, calls=%fused_computation.15 | convolution fusion | flops 926306304 | bytes 8257620 | tf_op jit(solution)/shard_map/ibcas,iasr->ibcr/dot_general | solution.py:90
  124.6 7.0 %collective-permute-start.17 = (f32[15,16,256]{2,1,0:T(8,128)S(1)}, f32[15,16,256]{2,1,0:T(8,128)S(1)}, u32[]{:S(2)}, u32[]{:S(2)}) collective-permute-start(f32[15,16,256]{2,1,0:T(8,128)S(1)} %pad_maximum_fusion.2), channel_id=1, source_target_pairs={{0,16},{16,32},{32,48},{48,64},{64,80},{80,96},{96,112},{112,128},... | collective-permute-start | bytes 737288 | tf_op jit(solution)/shard_map/ppermute | solution.py:36
  131.6 3.1 %collective-permute-done.17 = f32[15,16,256]{2,1,0:T(8,128)S(1)} collective-permute-done((f32[15,16,256]{2,1,0:T(8,128)S(1)}, f32[15,16,256]{2,1,0:T(8,128)S(1)}, u32[]{:S(2)}, u32[]{:S(2)}) %collective-permute-start.17) | collective-permute-done | bytes 245792 | tf_op jit(solution)/shard_map/ppermute | solution.py:36
  135.0 3.5 %collective-permute-done.18 = f32[15,16,256]{2,1,0:T(8,128)S(1)} collective-permute-done((f32[15,16,256]{2,1,0:T(8,128)S(1)}, f32[15,16,256]{2,1,0:T(8,128)S(1)}, u32[]{:S(2)}, u32[]{:S(2)}) %collective-permute-start.18) | collective-permute-done | bytes 245792 | tf_op jit(solution)/shard_map/ppermute | solution.py:36
  138.7 4.3 %fusion.2 = f32[3,7,16,256,1]{3,2,0,1,4:T(8,128)S(1)} fusion(f32[3,7,16,7,256]{4,2,1,0,3:T(8,128)S(1)} %fusion.58, f32[3,7,256,256]{3,2,1,0:T(8,128)} %constant_dynamic-update-slice_fusion, f32[3,7]{1,0:T(4,128)S(1)} %compare_convert_fusion), kind=kOutput, calls=%fused_computation.2 | convolution fusion | flops 926220288 | bytes 8257620 | tf_op jit(solution)/shard_map/ibcas,iasr->ibcr/dot_general | solution.py:90
  147.3 2.8 %collective-permute-done.19 = f32[15,16,256]{2,1,0:T(8,128)S(1)} collective-permute-done((f32[15,16,256]{2,1,0:T(8,128)S(1)}, f32[15,16,256]{2,1,0:T(8,128)S(1)}, u32[]{:S(2)}, u32[]{:S(2)}) %collective-permute-start.19) | collective-permute-done | bytes 245792 | tf_op jit(solution)/shard_map/ppermute | solution.py:36
  150.1 3.7 %collective-permute-done.20 = f32[15,16,256]{2,1,0:T(8,128)S(1)} collective-permute-done((f32[15,16,256]{2,1,0:T(8,128)S(1)}, f32[15,16,256]{2,1,0:T(8,128)S(1)}, u32[]{:S(2)}, u32[]{:S(2)}) %collective-permute-start.20) | collective-permute-done | bytes 245792 | tf_op jit(solution)/shard_map/ppermute | solution.py:36
  154.2 55.2 %all-gather.2.cloned.1.call-done = f32[3,7,256,256]{3,2,1,0:T(8,128)} async-done(((f32[3,7,16,256]{3,2,1,0:T(8,128)}), f32[3,7,256,256]{3,2,1,0:T(8,128)}) %all-gather.2.cloned.1.call-update) | async-done | bytes 5505040 | tf_op jit(solution)/shard_map/all_gather | solution.py:101
  209.5 4.4 %fusion.6 = f32[3,7,16,256,1]{3,2,0,1,4:T(8,128)S(1)} fusion(f32[3,7,16,7,256]{4,2,1,0,3:T(8,128)S(1)} %fusion.32, f32[3,7,256,256]{3,2,1,0:T(8,128)} %all-gather.2.cloned.1.call-done), kind=kOutput, calls=%fused_computation.6 | convolution fusion | flops 924844032 | bytes 8257536 | tf_op jit(solution)/shard_map/ibcas,iasr->ibcr/dot_general | solution.py:90
  214.1 3.1 %collective-permute-start.21 = (f32[15,16,256]{2,1,0:T(8,128)S(1)}, f32[15,16,256]{2,1,0:T(8,128)S(1)}, u32[]{:S(2)}, u32[]{:S(2)}) collective-permute-start(f32[15,16,256]{2,1,0:T(8,128)S(1)} %pad_maximum_fusion.6), channel_id=1, source_target_pairs={{0,16},{16,32},{32,48},{48,64},{64,80},{80,96},{96,112},{112,128},... | collective-permute-start | bytes 737288 | tf_op jit(solution)/shard_map/ppermute | solution.py:36
  217.2 3.1 %collective-permute-done.21 = f32[15,16,256]{2,1,0:T(8,128)S(1)} collective-permute-done((f32[15,16,256]{2,1,0:T(8,128)S(1)}, f32[15,16,256]{2,1,0:T(8,128)S(1)}, u32[]{:S(2)}, u32[]{:S(2)}) %collective-permute-start.21) | collective-permute-done | bytes 245792 | tf_op jit(solution)/shard_map/ppermute | solution.py:36
  220.6 3.4 %collective-permute-done.22 = f32[15,16,256]{2,1,0:T(8,128)S(1)} collective-permute-done((f32[15,16,256]{2,1,0:T(8,128)S(1)}, f32[15,16,256]{2,1,0:T(8,128)S(1)}, u32[]{:S(2)}, u32[]{:S(2)}) %collective-permute-start.22) | collective-permute-done | bytes 245792 | tf_op jit(solution)/shard_map/ppermute | solution.py:36
  (144 shorter events, 31.1 us)
Async XLA Ops:
  6.5 202.9 %all-gather.2.cloned.1.call-start = ((), (), s32[]{:S(2)}) async-start(), calls=%async_computation | async-start | bytes 5849088 | tf_op jit(solution)/shard_map/all_gather | solution.py:101
  7.3 3.0 %copy-start.1 = (f32[3,7,16,256]{3,2,1,0:T(8,128)S(1)}, f32[3,7,16,256]{3,2,1,0:T(8,128)}, u32[]{:S(2)}) copy-start(f32[3,7,16,256]{3,2,1,0:T(8,128)} %param.2) | copy-start | bytes 1032196
  11.2 12.5 %collective-permute-start = (f32[15,16,256]{2,1,0:T(8,128)S(1)}, f32[15,16,256]{2,1,0:T(8,128)S(1)}, u32[]{:S(2)}, u32[]{:S(2)}) collective-permute-start(f32[15,16,256]{2,1,0:T(8,128)S(1)} %pad_maximum_fusion), channel_id=1, source_target_pairs={{0,16},{16,32},{32,48},{48,64},{64,80},{80,96},{96,112},{112,128},... | collective-permute-start | bytes 737288 | tf_op jit(solution)/shard_map/ppermute | solution.py:36
  14.7 12.7 %collective-permute-start.2 = (f32[3,7,16,256]{3,2,1,0:T(8,128)S(1)}, f32[3,7,16,256]{3,2,1,0:T(8,128)S(1)}, u32[]{:S(2)}, u32[]{:S(2)}) collective-permute-start(f32[3,7,16,256]{3,2,1,0:T(8,128)S(1)} %copy-done.1), channel_id=1, source_target_pairs={{0,1},{1,2},{2,3},{3,4},{4,5},{5,6},{6,7},{7,8},{8,9},{9,10},{10,1... | collective-permute-start | bytes 1032200 | tf_op jit(solution)/shard_map/ppermute | solution.py:22
  17.8 12.5 %collective-permute-start.3 = (f32[3,7,16,256]{3,2,1,0:T(8,128)S(1)}, f32[3,7,16,256]{3,2,1,0:T(8,128)S(1)}, u32[]{:S(2)}, u32[]{:S(2)}) collective-permute-start(f32[3,7,16,256]{3,2,1,0:T(8,128)S(1)} %copy-done.1), channel_id=1, source_target_pairs={{0,15},{1,0},{2,1},{3,2},{4,3},{5,4},{6,5},{7,6},{8,7},{9,8},{10,9... | collective-permute-start | bytes 1032200 | tf_op jit(solution)/shard_map/ppermute | solution.py:27
  23.4 12.9 %copy-start.2 = (pred[7]{0:T(512)(128)(4,1)S(1)}, pred[7]{0:T(512)(128)(4,1)}, u32[]{:S(2)}) copy-start(pred[7]{0:T(512)(128)(4,1)} %constant.104.clone.1) | copy-start | bytes 25
  23.4 6.8 %collective-permute-start.1 = (f32[15,16,256]{2,1,0:T(8,128)S(1)}, f32[15,16,256]{2,1,0:T(8,128)S(1)}, u32[]{:S(2)}, u32[]{:S(2)}) collective-permute-start(f32[15,16,256]{2,1,0:T(8,128)S(1)} %pad_maximum_fusion.1), channel_id=1, source_target_pairs={{0,496},{16,0},{32,16},{48,32},{64,48},{80,64},{96,80},{112,96},{1... | collective-permute-start | bytes 737288 | tf_op jit(solution)/shard_map/ppermute | solution.py:36
  27.4 13.7 %collective-permute-start.4 = (f32[3,7,16,256]{3,2,1,0:T(8,128)S(1)}, f32[3,7,16,256]{3,2,1,0:T(8,128)S(1)}, u32[]{:S(2)}, u32[]{:S(2)}) collective-permute-start(f32[3,7,16,256]{3,2,1,0:T(8,128)S(1)} %collective-permute-done.2), channel_id=1, source_target_pairs={{0,1},{1,2},{2,3},{3,4},{4,5},{5,6},{6,7},{7,8},{8,9},{9,10},{10,1... | collective-permute-start | bytes 1032200 | tf_op jit(solution)/shard_map/ppermute | solution.py:22
  30.3 12.8 %collective-permute-start.5 = (f32[3,7,16,256]{3,2,1,0:T(8,128)S(1)}, f32[3,7,16,256]{3,2,1,0:T(8,128)S(1)}, u32[]{:S(2)}, u32[]{:S(2)}) collective-permute-start(f32[3,7,16,256]{3,2,1,0:T(8,128)S(1)} %collective-permute-done.3), channel_id=1, source_target_pairs={{0,15},{1,0},{2,1},{3,2},{4,3},{5,4},{6,5},{7,6},{8,7},{9,8},{10,9... | collective-permute-start | bytes 1032200 | tf_op jit(solution)/shard_map/ppermute | solution.py:27
  41.1 14.9 %collective-permute-start.6 = (f32[3,7,16,256]{3,2,1,0:T(8,128)S(1)}, f32[3,7,16,256]{3,2,1,0:T(8,128)S(1)}, u32[]{:S(2)}, u32[]{:S(2)}) collective-permute-start(f32[3,7,16,256]{3,2,1,0:T(8,128)S(1)} %collective-permute-done.4), channel_id=1, source_target_pairs={{0,1},{1,2},{2,3},{3,4},{4,5},{5,6},{6,7},{7,8},{8,9},{9,10},{10,1... | collective-permute-start | bytes 1032200 | tf_op jit(solution)/shard_map/ppermute | solution.py:22
  43.1 15.6 %collective-permute-start.7 = (f32[3,7,16,256]{3,2,1,0:T(8,128)S(1)}, f32[3,7,16,256]{3,2,1,0:T(8,128)S(1)}, u32[]{:S(2)}, u32[]{:S(2)}) collective-permute-start(f32[3,7,16,256]{3,2,1,0:T(8,128)S(1)} %collective-permute-done.5), channel_id=1, source_target_pairs={{0,15},{1,0},{2,1},{3,2},{4,3},{5,4},{6,5},{7,6},{8,7},{9,8},{10,9... | collective-permute-start | bytes 1032200 | tf_op jit(solution)/shard_map/ppermute | solution.py:27
  56.0 14.4 %collective-permute-start.8 = (f32[3,7,16,256]{3,2,1,0:T(8,128)S(1)}, f32[3,7,16,256]{3,2,1,0:T(8,128)S(1)}, u32[]{:S(2)}, u32[]{:S(2)}) collective-permute-start(f32[3,7,16,256]{3,2,1,0:T(8,128)S(1)} %collective-permute-done.6), channel_id=1, source_target_pairs={{0,1},{1,2},{2,3},{3,4},{4,5},{5,6},{6,7},{7,8},{8,9},{9,10},{10,1... | collective-permute-start | bytes 1032200 | tf_op jit(solution)/shard_map/ppermute | solution.py:22
  58.7 15.2 %collective-permute-start.9 = (f32[3,7,16,256]{3,2,1,0:T(8,128)S(1)}, f32[3,7,16,256]{3,2,1,0:T(8,128)S(1)}, u32[]{:S(2)}, u32[]{:S(2)}) collective-permute-start(f32[3,7,16,256]{3,2,1,0:T(8,128)S(1)} %collective-permute-done.7), channel_id=1, source_target_pairs={{0,15},{1,0},{2,1},{3,2},{4,3},{5,4},{6,5},{7,6},{8,7},{9,8},{10,9... | collective-permute-start | bytes 1032200 | tf_op jit(solution)/shard_map/ppermute | solution.py:27
  70.4 13.5 %collective-permute-start.10 = (f32[3,7,16,256]{3,2,1,0:T(8,128)S(1)}, f32[3,7,16,256]{3,2,1,0:T(8,128)S(1)}, u32[]{:S(2)}, u32[]{:S(2)}) collective-permute-start(f32[3,7,16,256]{3,2,1,0:T(8,128)S(1)} %collective-permute-done.8), channel_id=1, source_target_pairs={{0,1},{1,2},{2,3},{3,4},{4,5},{5,6},{6,7},{7,8},{8,9},{9,10},{10,1... | collective-permute-start | bytes 1032200 | tf_op jit(solution)/shard_map/ppermute | solution.py:22
  73.9 13.5 %collective-permute-start.11 = (f32[3,7,16,256]{3,2,1,0:T(8,128)S(1)}, f32[3,7,16,256]{3,2,1,0:T(8,128)S(1)}, u32[]{:S(2)}, u32[]{:S(2)}) collective-permute-start(f32[3,7,16,256]{3,2,1,0:T(8,128)S(1)} %collective-permute-done.9), channel_id=1, source_target_pairs={{0,15},{1,0},{2,1},{3,2},{4,3},{5,4},{6,5},{7,6},{8,7},{9,8},{10,9... | collective-permute-start | bytes 1032200 | tf_op jit(solution)/shard_map/ppermute | solution.py:27
  83.9 12.6 %collective-permute-start.12 = (f32[3,7,16,256]{3,2,1,0:T(8,128)S(1)}, f32[3,7,16,256]{3,2,1,0:T(8,128)S(1)}, u32[]{:S(2)}, u32[]{:S(2)}) collective-permute-start(f32[3,7,16,256]{3,2,1,0:T(8,128)S(1)} %collective-permute-done.10), channel_id=1, source_target_pairs={{0,1},{1,2},{2,3},{3,4},{4,5},{5,6},{6,7},{7,8},{8,9},{9,10},{10,1... | collective-permute-start | bytes 1032200 | tf_op jit(solution)/shard_map/ppermute | solution.py:22
  87.4 12.6 %collective-permute-start.13 = (f32[3,7,16,256]{3,2,1,0:T(8,128)S(1)}, f32[3,7,16,256]{3,2,1,0:T(8,128)S(1)}, u32[]{:S(2)}, u32[]{:S(2)}) collective-permute-start(f32[3,7,16,256]{3,2,1,0:T(8,128)S(1)} %collective-permute-done.11), channel_id=1, source_target_pairs={{0,15},{1,0},{2,1},{3,2},{4,3},{5,4},{6,5},{7,6},{8,7},{9,8},{10,9... | collective-permute-start | bytes 1032200 | tf_op jit(solution)/shard_map/ppermute | solution.py:27
  96.5 11.7 %collective-permute-start.14 = (f32[3,7,16,256]{3,2,1,0:T(8,128)S(1)}, f32[3,7,16,256]{3,2,1,0:T(8,128)S(1)}, u32[]{:S(2)}, u32[]{:S(2)}) collective-permute-start(f32[3,7,16,256]{3,2,1,0:T(8,128)S(1)} %collective-permute-done.12), channel_id=1, source_target_pairs={{0,1},{1,2},{2,3},{3,4},{4,5},{5,6},{6,7},{7,8},{8,9},{9,10},{10,1... | collective-permute-start | bytes 1032200 | tf_op jit(solution)/shard_map/ppermute | solution.py:22
  100.0 11.9 %collective-permute-start.15 = (f32[3,7,16,256]{3,2,1,0:T(8,128)S(1)}, f32[3,7,16,256]{3,2,1,0:T(8,128)S(1)}, u32[]{:S(2)}, u32[]{:S(2)}) collective-permute-start(f32[3,7,16,256]{3,2,1,0:T(8,128)S(1)} %collective-permute-done.13), channel_id=1, source_target_pairs={{0,15},{1,0},{2,1},{3,2},{4,3},{5,4},{6,5},{7,6},{8,7},{9,8},{10,9... | collective-permute-start | bytes 1032200 | tf_op jit(solution)/shard_map/ppermute | solution.py:27
  108.2 11.3 %collective-permute-start.16 = (f32[3,7,16,256]{3,2,1,0:T(8,128)S(1)}, f32[3,7,16,256]{3,2,1,0:T(8,128)S(1)}, u32[]{:S(2)}, u32[]{:S(2)}) collective-permute-start(f32[3,7,16,256]{3,2,1,0:T(8,128)S(1)} %collective-permute-done.14), channel_id=1, source_target_pairs={{0,1},{1,2},{2,3},{3,4},{4,5},{5,6},{6,7},{7,8},{8,9},{9,10},{10,1... | collective-permute-start | bytes 1032200 | tf_op jit(solution)/shard_map/ppermute | solution.py:22
  124.6 10.1 %collective-permute-start.17 = (f32[15,16,256]{2,1,0:T(8,128)S(1)}, f32[15,16,256]{2,1,0:T(8,128)S(1)}, u32[]{:S(2)}, u32[]{:S(2)}) collective-permute-start(f32[15,16,256]{2,1,0:T(8,128)S(1)} %pad_maximum_fusion.2), channel_id=1, source_target_pairs={{0,16},{16,32},{32,48},{48,64},{64,80},{80,96},{96,112},{112,128},... | collective-permute-start | bytes 737288 | tf_op jit(solution)/shard_map/ppermute | solution.py:36
  131.6 6.8 %collective-permute-start.18 = (f32[15,16,256]{2,1,0:T(8,128)S(1)}, f32[15,16,256]{2,1,0:T(8,128)S(1)}, u32[]{:S(2)}, u32[]{:S(2)}) collective-permute-start(f32[15,16,256]{2,1,0:T(8,128)S(1)} %pad_maximum_fusion.3), channel_id=1, source_target_pairs={{0,496},{16,0},{32,16},{48,32},{64,48},{80,64},{96,80},{112,96},{1... | collective-permute-start | bytes 737288 | tf_op jit(solution)/shard_map/ppermute | solution.py:36
  143.8 10.1 %copy-start = (f32[3,7,16,256]{3,2,1,0:T(8,128)S(1)}, f32[3,7,16,256]{3,2,1,0:T(8,128)}, u32[]{:S(2)}) copy-start(f32[3,7,16,256]{3,2,1,0:T(8,128)} %fusion.80) | copy-start | bytes 1032196
  146.7 3.4 %collective-permute-start.19 = (f32[15,16,256]{2,1,0:T(8,128)S(1)}, f32[15,16,256]{2,1,0:T(8,128)S(1)}, u32[]{:S(2)}, u32[]{:S(2)}) collective-permute-start(f32[15,16,256]{2,1,0:T(8,128)S(1)} %pad_maximum_fusion.4), channel_id=1, source_target_pairs={{0,16},{16,32},{32,48},{48,64},{64,80},{80,96},{96,112},{112,128},... | collective-permute-start | bytes 737288 | tf_op jit(solution)/shard_map/ppermute | solution.py:36
  147.0 6.8 %collective-permute-start.20 = (f32[15,16,256]{2,1,0:T(8,128)S(1)}, f32[15,16,256]{2,1,0:T(8,128)S(1)}, u32[]{:S(2)}, u32[]{:S(2)}) collective-permute-start(f32[15,16,256]{2,1,0:T(8,128)S(1)} %pad_maximum_fusion.5), channel_id=1, source_target_pairs={{0,496},{16,0},{32,16},{48,32},{64,48},{80,64},{96,80},{112,96},{1... | collective-permute-start | bytes 737288 | tf_op jit(solution)/shard_map/ppermute | solution.py:36
  209.5 14.8 %slice-start = ((s8[5505024]{0:T(1024)(128)(4,1)}), s8[4194304]{0:T(1024)(128)(4,1)S(1)}, s32[]{:S(2)}) async-start(s8[5505024]{0:T(1024)(128)(4,1)} %bitcast.255), calls=%async_computation.1 | async-start | bytes 8388608
  214.0 10.3 %slice-start.1 = ((s8[5505024]{0:T(1024)(128)(4,1)}), s8[1310720]{0:T(1024)(128)(4,1)S(1)}, s32[]{:S(2)}) async-start(s8[5505024]{0:T(1024)(128)(4,1)} %bitcast.255), calls=%async_computation.2 | async-start | bytes 2621440
  214.1 6.2 %collective-permute-start.21 = (f32[15,16,256]{2,1,0:T(8,128)S(1)}, f32[15,16,256]{2,1,0:T(8,128)S(1)}, u32[]{:S(2)}, u32[]{:S(2)}) collective-permute-start(f32[15,16,256]{2,1,0:T(8,128)S(1)} %pad_maximum_fusion.6), channel_id=1, source_target_pairs={{0,16},{16,32},{32,48},{48,64},{64,80},{80,96},{96,112},{112,128},... | collective-permute-start | bytes 737288 | tf_op jit(solution)/shard_map/ppermute | solution.py:36
  217.2 6.8 %collective-permute-start.22 = (f32[15,16,256]{2,1,0:T(8,128)S(1)}, f32[15,16,256]{2,1,0:T(8,128)S(1)}, u32[]{:S(2)}, u32[]{:S(2)}) collective-permute-start(f32[15,16,256]{2,1,0:T(8,128)S(1)} %pad_maximum_fusion.7), channel_id=1, source_target_pairs={{0,496},{16,0},{32,16},{48,32},{64,48},{80,64},{96,80},{112,96},{1... | collective-permute-start | bytes 737288 | tf_op jit(solution)/shard_map/ppermute | solution.py:36
Sparse Core Ops, SparseCore 0:
  143.9 65.4 all-gather.1
